TPU v7x, 256 devices: a whole 4x4x8 slice. The times are simulated.
256 devices in a mesh: req: 32 (over z_hi, x, y), tp: 8 (over z_lo, core).
Axes of the slice: x: 4, y: 4, z: 8 (z_hi: 2, z_lo: 4; z = z_hi * 4 + z_lo), core: 2. Of those that a mesh axis runs over, the one named last changes fastest.
Arguments:
- tokens: bfloat16 [8192, 2560], P('req'), may hold values from -6 to 6
- norm_gain: float32 [2560], replicated, may hold values from 0.1 to 1.9
- w_query: bfloat16 [2560, 2560], P(None, 'tp')
- w_key: bfloat16 [2560, 640], P(None, 'tp')
- w_value: bfloat16 [2560, 640], P(None, 'tp'), may hold values from -0.125 to 0.125
- page_counts: int32 [16], replicated, may hold values from 1 to 128, 512 in all
- pad_counts: int32 [16], replicated, may hold values from 0 to 15
- page_table: int32 [32, 16], P('req'), may hold values from 0 to 15, each once within a row
Outputs:
- context: bfloat16 [8192, 2560], P('req', 'tp')
- cache: bfloat16 [512, 8, 2560], P(('req', 'tp'))
Inputs may be any that keep to these rules, and one draw needn't show every extreme that they name: `page_counts`: each prompt has at least one live slot; the slots of all prompts fill the stream exactly. `page_table`: each row is a permutation; cache slot s of a block belongs to tp index s // 2.
All inputs are finite; a program needn't handle non-finite values.
Results may differ from a plain program's by a relative error of at most 0.012.
Values may be sent and summed in bfloat16 or wider, within the bound.
No kernel may reach another device: no remote copies, remote signals or barrier semaphores. Data moves between devices by JAX's collectives and lax.ppermute only.
A program may use at most 64 MiB of HBM per device.

v0:
```python
import jax
import jax.numpy as jnp
from jax import lax
from jax.sharding import PartitionSpec as P

HD = 80
WINDOW = 4096
PAGE = 16


NORM_EPS = 1e-05
ROPE_BASE = 10000.0
MASKED_SCORE = -1e30


def passed_along(x, axis, by):
    size = lax.axis_size(axis)
    pairs = [(i, i + by) for i in range(size) if 0 <= i + by < size]
    return lax.ppermute(x, axis, pairs)


def token_meta(slot_index, page_counts, pad_counts):
    prompt_count = page_counts.shape[0]
    slot_counts = page_counts * PAGE
    slot_ends = jnp.cumsum(slot_counts)
    segment_id = jnp.sum((slot_index[:, None] >= slot_ends[None, :]).astype(jnp.int32), axis=1)
    one_hot = (segment_id[:, None] == jnp.arange(prompt_count, dtype=jnp.int32)[None, :]).astype(
        jnp.int32
    )
    first_slot = jnp.sum(one_hot * (slot_ends - slot_counts)[None, :], axis=1)
    live_count = jnp.sum(one_hot * (slot_counts - pad_counts)[None, :], axis=1)
    position = slot_index - first_slot
    inside = slot_index >= 0
    is_live = (position < live_count) & inside
    segment_id = jnp.where(inside, segment_id, -1)
    return (segment_id, position, is_live)


def rotate(vectors, position):
    half_width = vectors.shape[-1] // 2
    frequency = ROPE_BASE ** (-2.0 * jnp.arange(half_width, dtype=jnp.float32) / vectors.shape[-1])
    angles = position.astype(jnp.float32)[:, None, None] * frequency[None, None, :]
    cosine = jnp.cos(angles)
    sine_part = jnp.sin(angles)
    front_half = vectors[..., :half_width]
    back_half = vectors[..., half_width:]
    return jnp.concatenate(
        [front_half * cosine - back_half * sine_part, back_half * cosine + front_half * sine_part],
        axis=-1,
    )


def project(tokens, norm_gain, w_query, w_key, w_value, position):
    row_count = tokens.shape[0]
    as_float = tokens.astype(jnp.float32)
    normed = (
        as_float
        * lax.rsqrt(jnp.mean(as_float * as_float, axis=-1, keepdims=True) + NORM_EPS)
        * norm_gain
    ).astype(jnp.bfloat16)
    query_rot = jnp.dot(normed, w_query, preferred_element_type=jnp.float32).reshape(
        row_count, -1, HD
    )
    query_rot = rotate(query_rot, position).astype(jnp.bfloat16)
    key_rot = jnp.dot(normed, w_key, preferred_element_type=jnp.float32).reshape(row_count, -1, HD)
    key_rot = rotate(key_rot, position).astype(jnp.bfloat16)
    value_rows = (
        jnp.dot(normed, w_value, preferred_element_type=jnp.float32)
        .reshape(row_count, -1, HD)
        .astype(jnp.bfloat16)
    )
    return (query_rot, key_rot, value_rows)


def per_device(tokens, norm_gain, w_query, w_key, w_value, page_counts, pad_counts, page_table):
    row_count = tokens.shape[0]
    stream_total = row_count * lax.axis_size("req")
    longest_prompt = min(8 * row_count, stream_total // 2)
    reach_blocks = min(WINDOW, longest_prompt) // row_count
    block_start = lax.axis_index("req") * row_count
    slot_index = block_start + jnp.arange(row_count, dtype=jnp.int32)
    segment_id, position, is_live = token_meta(slot_index, page_counts, pad_counts)
    query_rot, key_rot, value_rows = project(tokens, norm_gain, w_query, w_key, w_value, position)
    kv_heads = key_rot.shape[1]
    group_size = query_rot.shape[1] // kv_heads
    head_total = kv_heads * group_size
    packed = jnp.concatenate([key_rot, value_rows], axis=-1)

    def relay(held_block, unused):
        arrived = passed_along(held_block, "req", 1)
        return (arrived, arrived)

    unused_last, earlier_stack = lax.scan(relay, packed, None, length=reach_blocks)
    key_blocks = jnp.concatenate([earlier_stack[::-1], packed[None]], axis=0)
    key_index = (
        block_start
        - reach_blocks * row_count
        + jnp.arange((reach_blocks + 1) * row_count, dtype=jnp.int32)
    )
    key_segment, unused_position, key_live = token_meta(key_index, page_counts, pad_counts)
    key_index = key_index.reshape(reach_blocks + 1, row_count)
    key_segment = key_segment.reshape(reach_blocks + 1, row_count)
    key_live = key_live.reshape(reach_blocks + 1, row_count)
    allowed = (key_segment[:, None, :] == segment_id[None, :, None]) & key_live[:, None, :]
    allowed = (
        allowed
        & (key_index[:, None, :] <= slot_index[None, :, None])
        & (slot_index[None, :, None] - key_index[:, None, :] < WINDOW)
    )
    score_scale = HD ** (-0.5)

    def one_head(head_id):
        kv_id = head_id // group_size
        head_queries = lax.dynamic_index_in_dim(query_rot, head_id, 1, keepdims=False)
        head_kv = lax.dynamic_index_in_dim(key_blocks, kv_id, 2, keepdims=False)

        def score_tile(inputs):
            kv_block, block_allowed, block_segment = inputs
            tile = (
                lax.dot_general(
                    head_queries,
                    kv_block[:, :HD],
                    (((1,), (1,)), ((), ())),
                    preferred_element_type=jnp.float32,
                )
                * score_scale
            )
            return jnp.where(block_allowed, tile, MASKED_SCORE)

        scores = lax.map(score_tile, (head_kv, allowed, key_segment))
        row_max = jnp.max(jnp.max(scores, axis=-1), axis=0)

        def value_step(state, inputs):
            block_scores, kv_block, block_allowed, block_segment = inputs
            prob_total, weighted = state
            probs = jnp.where(block_allowed, jnp.exp(block_scores - row_max[:, None]), 0.0)
            weights = probs.astype(jnp.bfloat16)
            update = jnp.dot(weights, kv_block[:, HD:], preferred_element_type=jnp.float32)
            return ((prob_total + jnp.sum(probs, axis=-1), weighted + update), None)

        start_state = (
            jnp.zeros((row_count,), jnp.float32),
            jnp.zeros((row_count, HD), jnp.float32),
        )
        final_state, unused_rest = lax.scan(
            value_step, start_state, (scores, head_kv, allowed, key_segment)
        )
        prob_total, weighted = final_state
        return weighted / prob_total[:, None]

    per_head = lax.map(one_head, jnp.arange(head_total, dtype=jnp.int32))
    result = jnp.transpose(per_head, (1, 0, 2)).reshape(row_count, head_total * HD)
    context = jnp.where(is_live[:, None], result, 0.0).astype(jnp.bfloat16)
    live_rows = jnp.where(is_live[:, None, None], packed, jnp.zeros((), jnp.bfloat16))
    page_total = row_count // PAGE
    page_rows = (
        live_rows.reshape(page_total, PAGE, kv_heads, 2 * HD)
        .transpose(0, 2, 1, 3)
        .reshape(page_total, kv_heads, PAGE * 2 * HD)
    )
    tp_count = lax.axis_size("tp")
    slots_here = page_total // tp_count
    local_table = page_table[0]
    slot_hits = (local_table[None, :] == jnp.arange(page_total, dtype=jnp.int32)[:, None]).astype(
        jnp.int32
    )
    page_order = jnp.sum(slot_hits * jnp.arange(page_total, dtype=jnp.int32)[None, :], axis=1)
    page_order = page_order.reshape(tp_count, slots_here).T
    outgoing = page_rows[page_order].reshape(slots_here, tp_count * kv_heads, PAGE * 2 * HD)
    cache = lax.all_to_all(outgoing, "tp", split_axis=1, concat_axis=1, tiled=True)
    return (context, cache)


def solution(mesh):
    in_specs = (
        P("req", None),
        P(),
        P(None, "tp"),
        P(None, "tp"),
        P(None, "tp"),
        P(),
        P(),
        P("req", None),
    )
    out_specs = (P("req", "tp"), P(("req", "tp"), None, None))
    return jax.shard_map(
        per_device, mesh=mesh, in_specs=in_specs, out_specs=out_specs, check_vma=False
    )
```

profile of v0, /device:TPU:192, one launch (start us, length us, event | category | flops | bytes accessed | tf_op | source)
XLA Modules:
  0.0 348.5 jit_solution(8017598438472423055)
XLA Ops:
  3.2 1.7 fusion.18
  4.9 2.0 convolution_bitcast_fusion
  10.8 5.3 %all-to-all-start = ((bf16[2,8,2560]{2,0,1:T(2,128)(2,1)}), bf16[2,8,2560]{2,0,1:T(2,128)(2,1)}, u32[]{:S(2)}, u32[]{:S(2)}) async-start(bf16[2,8,2560]{2,0,1:T(2,128)(2,1)} %copy.48), calls=%async_computation | async-start | bytes 163840 | tf_op jit(solution)/shard_map/all_to_all | solution.py:170
  16.2 1.2 multiply_cosine_fusion
  18.1 1.4 select_reduce_fusion.1
  20.1 1.4 fusion.42
  21.8 1.0 copy.53
  22.8 122.8 %while.48 = (s32[]{:T(128)}, bf16[256,1,160]{0,2,1:T(8,128)(2,1)S(1)}, bf16[8,256,1,160]{1,3,2,0:T(8,128)(2,1)}, s32[]{:T(128)}) while((s32[]{:T(128)}, bf16[256,1,160]{0,2,1:T(8,128)(2,1)S(1)}, bf16[8,256,1,160]{1,3,2,0:T(8,128)(2,1)}, s32[]{:T(128)}) %tuple.111), condition=%wide.region_6.7_spmd, body=%wide.region_5.6_spmd.sunk | while | flops 2 | bytes 655465 | solution.py:93
  22.8 3.5 collective-permute-start
  26.3 12.6 %collective-permute-done = bf16[256,1,160]{0,2,1:T(8,128)(2,1)S(1)} collective-permute-done((bf16[256,1,160]{0,2,1:T(8,128)(2,1)S(1)}, bf16[256,1,160]{0,2,1:T(8,128)(2,1)S(1)}, u32[]{:S(2)}, u32[]{:S(2)}) %collective-permute-start) | collective-permute-done | bytes 81952 | tf_op jit(solution)/shard_map/while/body/eval_jaxpr/ppermute | solution.py:19
  39.5 1.9 collective-permute-start
  41.4 12.6 %collective-permute-done = bf16[256,1,160]{0,2,1:T(8,128)(2,1)S(1)} collective-permute-done((bf16[256,1,160]{0,2,1:T(8,128)(2,1)S(1)}, bf16[256,1,160]{0,2,1:T(8,128)(2,1)S(1)}, u32[]{:S(2)}, u32[]{:S(2)}) %collective-permute-start) | collective-permute-done | bytes 81952 | tf_op jit(solution)/shard_map/while/body/eval_jaxpr/ppermute | solution.py:19
  54.6 1.9 collective-permute-start
  56.6 12.5 %collective-permute-done = bf16[256,1,160]{0,2,1:T(8,128)(2,1)S(1)} collective-permute-done((bf16[256,1,160]{0,2,1:T(8,128)(2,1)S(1)}, bf16[256,1,160]{0,2,1:T(8,128)(2,1)S(1)}, u32[]{:S(2)}, u32[]{:S(2)}) %collective-permute-start) | collective-permute-done | bytes 81952 | tf_op jit(solution)/shard_map/while/body/eval_jaxpr/ppermute | solution.py:19
  69.8 1.9 collective-permute-start
  71.7 12.6 %collective-permute-done = bf16[256,1,160]{0,2,1:T(8,128)(2,1)S(1)} collective-permute-done((bf16[256,1,160]{0,2,1:T(8,128)(2,1)S(1)}, bf16[256,1,160]{0,2,1:T(8,128)(2,1)S(1)}, u32[]{:S(2)}, u32[]{:S(2)}) %collective-permute-start) | collective-permute-done | bytes 81952 | tf_op jit(solution)/shard_map/while/body/eval_jaxpr/ppermute | solution.py:19
  84.9 1.9 collective-permute-start
  86.8 12.6 %collective-permute-done = bf16[256,1,160]{0,2,1:T(8,128)(2,1)S(1)} collective-permute-done((bf16[256,1,160]{0,2,1:T(8,128)(2,1)S(1)}, bf16[256,1,160]{0,2,1:T(8,128)(2,1)S(1)}, u32[]{:S(2)}, u32[]{:S(2)}) %collective-permute-start) | collective-permute-done | bytes 81952 | tf_op jit(solution)/shard_map/while/body/eval_jaxpr/ppermute | solution.py:19
  100.0 1.9 collective-permute-start
  101.9 12.6 %collective-permute-done = bf16[256,1,160]{0,2,1:T(8,128)(2,1)S(1)} collective-permute-done((bf16[256,1,160]{0,2,1:T(8,128)(2,1)S(1)}, bf16[256,1,160]{0,2,1:T(8,128)(2,1)S(1)}, u32[]{:S(2)}, u32[]{:S(2)}) %collective-permute-start) | collective-permute-done | bytes 81952 | tf_op jit(solution)/shard_map/while/body/eval_jaxpr/ppermute | solution.py:19
  115.2 1.9 collective-permute-start
  117.1 12.6 %collective-permute-done = bf16[256,1,160]{0,2,1:T(8,128)(2,1)S(1)} collective-permute-done((bf16[256,1,160]{0,2,1:T(8,128)(2,1)S(1)}, bf16[256,1,160]{0,2,1:T(8,128)(2,1)S(1)}, u32[]{:S(2)}, u32[]{:S(2)}) %collective-permute-start) | collective-permute-done | bytes 81952 | tf_op jit(solution)/shard_map/while/body/eval_jaxpr/ppermute | solution.py:19
  130.4 1.9 collective-permute-start
  132.3 12.6 %collective-permute-done = bf16[256,1,160]{0,2,1:T(8,128)(2,1)S(1)} collective-permute-done((bf16[256,1,160]{0,2,1:T(8,128)(2,1)S(1)}, bf16[256,1,160]{0,2,1:T(8,128)(2,1)S(1)}, u32[]{:S(2)}, u32[]{:S(2)}) %collective-permute-start) | collective-permute-done | bytes 81952 | tf_op jit(solution)/shard_map/while/body/eval_jaxpr/ppermute | solution.py:19
  145.6 2.2 copy.42
  147.8 1.3 rev.3
  152.0 1.2 subtract_convert_fusion
  153.4 1.2 pad_maximum_fusion
  154.6 190.7 %while.51 = (s32[]{:T(128)}, bf16[4,256,80]{1,2,0:T(8,128)(2,1)}, bf16[9,256,1,160]{3,1,0,2:T(8,128)(2,1)}, s32[4]{0:T(128)S(1)}, bf16[256,4,80]{2,0,1:T(8,128)(...) while((s32[]{:T(128)}, bf16[4,256,80]{1,2,0:T(8,128)(2,1)}, ...), condition=%wide.region_17.18_spmd.clone, body=%wide.region_10.17_spmd.clone.sunk | while | flops 26275848 | bytes 7519580 | solution.py:151
  157.2 1.2 fusion.58
  158.4 17.9 %while.52 = (s32[]{:T(128)}, f32[9,256,256]{1,2,0:T(8,128)}, pred[9,256,256]{2,1,0:T(32,128)(4,1)S(1)}, bf16[9,256,160]{2,1,0:T(8,128)(2,1)}, bf16[256,80]{1,0:T(8,128)(2,1)S(1)}, /*index=5*/s32[]{:T(128)}) while((s32[]{:T(128)}, f32[9,256,256]{1,2,0:T(8,128)}, pred[9,256,256]{2,1,0:T(32,128)(4,1)S(1)}, bf16[9,256,160]{2,1,0:T(8,128)(2,1)}, ...), condition=%wide.region_12.12_spmd, body=%wide.region_11.11_spmd.sunk | while | flops 10616834 | bytes 885325 | solution.py:130
  176.3 2.0 reduce_max.13
  178.3 23.3 %while.53 = (s32[]{:T(128)}, f32[256]{0:T(256)S(1)}, f32[256,80]{0,1:T(8,128)S(1)}, pred[9,256,256]{2,1,0:T(32,128)(4,1)S(1)}, f32[9,256,256]{1,2,0:T(8,128)}, /...) while((s32[]{:T(128)}, f32[256]{0:T(256)S(1)}, ...), condition=%wide.region_16.16_spmd.clone, body=%wide.region_14.15_spmd.clone.sunk | while | flops 10920195 | bytes 2103416 | solution.py:145
  178.3 1.0 constant_dynamic-slice_fusion.5
  180.9 1.0 constant_dynamic-slice_fusion.5
  183.5 1.0 constant_dynamic-slice_fusion.5
  186.1 1.0 constant_dynamic-slice_fusion.5
  188.7 1.0 constant_dynamic-slice_fusion.5
  191.3 1.0 constant_dynamic-slice_fusion.5
  193.9 1.0 constant_dynamic-slice_fusion.5
  196.5 1.0 constant_dynamic-slice_fusion.5
  199.0 1.0 constant_dynamic-slice_fusion.5
  204.9 1.2 fusion.58
  206.0 17.9 %while.52 = (s32[]{:T(128)}, f32[9,256,256]{1,2,0:T(8,128)}, pred[9,256,256]{2,1,0:T(32,128)(4,1)S(1)}, bf16[9,256,160]{2,1,0:T(8,128)(2,1)}, bf16[256,80]{1,0:T(8,128)(2,1)S(1)}, /*index=5*/s32[]{:T(128)}) while((s32[]{:T(128)}, f32[9,256,256]{1,2,0:T(8,128)}, pred[9,256,256]{2,1,0:T(32,128)(4,1)S(1)}, bf16[9,256,160]{2,1,0:T(8,128)(2,1)}, ...), condition=%wide.region_12.12_spmd, body=%wide.region_11.11_spmd.sunk | while | flops 10616834 | bytes 885325 | solution.py:130
  223.9 2.0 reduce_max.13
  225.9 23.3 %while.53 = (s32[]{:T(128)}, f32[256]{0:T(256)S(1)}, f32[256,80]{0,1:T(8,128)S(1)}, pred[9,256,256]{2,1,0:T(32,128)(4,1)S(1)}, f32[9,256,256]{1,2,0:T(8,128)}, /...) while((s32[]{:T(128)}, f32[256]{0:T(256)S(1)}, ...), condition=%wide.region_16.16_spmd.clone, body=%wide.region_14.15_spmd.clone.sunk | while | flops 10920195 | bytes 2103416 | solution.py:145
  226.0 1.0 constant_dynamic-slice_fusion.5
  231.2 1.0 constant_dynamic-slice_fusion.5
  233.8 1.0 constant_dynamic-slice_fusion.5
  236.4 1.0 constant_dynamic-slice_fusion.5
  238.9 1.0 constant_dynamic-slice_fusion.5
  241.5 1.0 constant_dynamic-slice_fusion.5
  252.5 1.2 fusion.58
  253.7 17.9 %while.52 = (s32[]{:T(128)}, f32[9,256,256]{1,2,0:T(8,128)}, pred[9,256,256]{2,1,0:T(32,128)(4,1)S(1)}, bf16[9,256,160]{2,1,0:T(8,128)(2,1)}, bf16[256,80]{1,0:T(8,128)(2,1)S(1)}, /*index=5*/s32[]{:T(128)}) while((s32[]{:T(128)}, f32[9,256,256]{1,2,0:T(8,128)}, pred[9,256,256]{2,1,0:T(32,128)(4,1)S(1)}, bf16[9,256,160]{2,1,0:T(8,128)(2,1)}, ...), condition=%wide.region_12.12_spmd, body=%wide.region_11.11_spmd.sunk | while | flops 10616834 | bytes 885325 | solution.py:130
  271.6 2.0 reduce_max.13
  273.6 23.3 %while.53 = (s32[]{:T(128)}, f32[256]{0:T(256)S(1)}, f32[256,80]{0,1:T(8,128)S(1)}, pred[9,256,256]{2,1,0:T(32,128)(4,1)S(1)}, f32[9,256,256]{1,2,0:T(8,128)}, /...) while((s32[]{:T(128)}, f32[256]{0:T(256)S(1)}, ...), condition=%wide.region_16.16_spmd.clone, body=%wide.region_14.15_spmd.clone.sunk | while | flops 10920195 | bytes 2103416 | solution.py:145
  273.6 1.0 constant_dynamic-slice_fusion.5
  300.2 1.2 fusion.58
  301.4 17.9 %while.52 = (s32[]{:T(128)}, f32[9,256,256]{1,2,0:T(8,128)}, pred[9,256,256]{2,1,0:T(32,128)(4,1)S(1)}, bf16[9,256,160]{2,1,0:T(8,128)(2,1)}, bf16[256,80]{1,0:T(8,128)(2,1)S(1)}, /*index=5*/s32[]{:T(128)}) while((s32[]{:T(128)}, f32[9,256,256]{1,2,0:T(8,128)}, pred[9,256,256]{2,1,0:T(32,128)(4,1)S(1)}, bf16[9,256,160]{2,1,0:T(8,128)(2,1)}, ...), condition=%wide.region_12.12_spmd, body=%wide.region_11.11_spmd.sunk | while | flops 10616834 | bytes 885325 | solution.py:130
  319.3 2.0 reduce_max.13
  321.3 23.3 %while.53 = (s32[]{:T(128)}, f32[256]{0:T(256)S(1)}, f32[256,80]{0,1:T(8,128)S(1)}, pred[9,256,256]{2,1,0:T(32,128)(4,1)S(1)}, f32[9,256,256]{1,2,0:T(8,128)}, /...) while((s32[]{:T(128)}, f32[256]{0:T(256)S(1)}, ...), condition=%wide.region_16.16_spmd.clone, body=%wide.region_14.15_spmd.clone.sunk | while | flops 10920195 | bytes 2103416 | solution.py:145
  321.3 1.0 constant_dynamic-slice_fusion.5
  345.3 1.6 fusion.22
  346.9 1.5 copy.49
  (478 shorter events, 167.2 us)
Async XLA Ops:
  0.6 19.5 %copy-start = (bf16[2560,320]{0,1:T(8,128)(2,1)S(1)}, bf16[2560,320]{0,1:T(8,128)(2,1)}, u32[]{:S(2)}) copy-start(bf16[2560,320]{0,1:T(8,128)(2,1)} %param.18) | copy-start | bytes 4915204
  0.6 6.2 %copy-start.1 = (bf16[256,2560]{1,0:T(8,128)(2,1)S(1)}, bf16[256,2560]{1,0:T(8,128)(2,1)}, u32[]{:S(2)}) copy-start(bf16[256,2560]{1,0:T(8,128)(2,1)} %param.16) | copy-start | bytes 3932164
  0.7 6.2 %copy-start.19 = (f32[2560]{0:T(1024)S(1)}, f32[2560]{0:T(1024)}, u32[]{:S(2)}) copy-start(f32[2560]{0:T(1024)} %param.17) | copy-start | bytes 30724
  0.7 6.2 %copy-start.18 = (bf16[2560,80]{0,1:T(8,128)(2,1)S(1)}, bf16[2560,80]{0,1:T(8,128)(2,1)}, u32[]{:S(2)}) copy-start(bf16[2560,80]{0,1:T(8,128)(2,1)} %param.20) | copy-start | bytes 1228804
  0.7 6.9 %copy-start.16 = (f32[40]{0:T(128)}, f32[40]{0:T(128)S(1)}, u32[]{:S(2)}) copy-start(f32[40]{0:T(128)S(1)} %multiply_power_fusion) | copy-start | bytes 484
  0.7 6.8 %copy-start.7 = (s32[256]{0:T(256)}, s32[256]{0:T(256)S(1)}, u32[]{:S(2)}) copy-start(s32[256]{0:T(256)S(1)} %iota_add_fusion.1) | copy-start | bytes 3076
  1.8 0.9 copy-start.11
  2.6 5.0 %copy-start.14 = (s32[16]{0:T(128)}, s32[16]{0:T(128)S(1)}, u32[]{:S(2)}) copy-start(s32[16]{0:T(128)S(1)} %get-tuple-element.298) | copy-start | bytes 196
  2.6 5.0 %copy-start.15 = (s32[16]{0:T(128)}, s32[16]{0:T(128)S(1)}, u32[]{:S(2)}) copy-start(s32[16]{0:T(128)S(1)} %get-tuple-element.299) | copy-start | bytes 196
  3.2 4.4 %copy-start.10 = (f32[256]{0:T(256)}, f32[256]{0:T(256)S(1)}, u32[]{:S(2)}) copy-start(f32[256]{0:T(256)S(1)} %get-tuple-element.301) | copy-start | bytes 3076
  4.9 2.7 copy-start.17
  7.6 3.3 copy-start.12
  7.8 1.6 copy-start.3
  10.8 336.1 %all-to-all-start = ((bf16[2,8,2560]{2,0,1:T(2,128)(2,1)}), bf16[2,8,2560]{2,0,1:T(2,128)(2,1)}, u32[]{:S(2)}, u32[]{:S(2)}) async-start(bf16[2,8,2560]{2,0,1:T(2,128)(2,1)} %copy.48), calls=%async_computation | async-start | bytes 163840 | tf_op jit(solution)/shard_map/all_to_all | solution.py:170
  20.1 2.7 copy-start.4
  22.8 16.0 %collective-permute-start = (bf16[256,1,160]{0,2,1:T(8,128)(2,1)S(1)}, bf16[256,1,160]{0,2,1:T(8,128)(2,1)S(1)}, u32[]{:S(2)}, u32[]{:S(2)}) collective-permute-start(bf16[256,1,160]{0,2,1:T(8,128)(2,1)S(1)} %get-tuple-element.539), channel_id=1, source_target_pairs={{0,8},{8,16},{16,24},{24,32},{32,40},{40,48},{48,56},{56,64},{64,7... | collective-permute-start | bytes 245768 | tf_op jit(solution)/shard_map/while/body/eval_jaxpr/ppermute | solution.py:19
  39.5 14.5 %collective-permute-start = (bf16[256,1,160]{0,2,1:T(8,128)(2,1)S(1)}, bf16[256,1,160]{0,2,1:T(8,128)(2,1)S(1)}, u32[]{:S(2)}, u32[]{:S(2)}) collective-permute-start(bf16[256,1,160]{0,2,1:T(8,128)(2,1)S(1)} %get-tuple-element.539), channel_id=1, source_target_pairs={{0,8},{8,16},{16,24},{24,32},{32,40},{40,48},{48,56},{56,64},{64,7... | collective-permute-start | bytes 245768 | tf_op jit(solution)/shard_map/while/body/eval_jaxpr/ppermute | solution.py:19
  54.6 14.5 %collective-permute-start = (bf16[256,1,160]{0,2,1:T(8,128)(2,1)S(1)}, bf16[256,1,160]{0,2,1:T(8,128)(2,1)S(1)}, u32[]{:S(2)}, u32[]{:S(2)}) collective-permute-start(bf16[256,1,160]{0,2,1:T(8,128)(2,1)S(1)} %get-tuple-element.539), channel_id=1, source_target_pairs={{0,8},{8,16},{16,24},{24,32},{32,40},{40,48},{48,56},{56,64},{64,7... | collective-permute-start | bytes 245768 | tf_op jit(solution)/shard_map/while/body/eval_jaxpr/ppermute | solution.py:19
  69.8 14.5 %collective-permute-start = (bf16[256,1,160]{0,2,1:T(8,128)(2,1)S(1)}, bf16[256,1,160]{0,2,1:T(8,128)(2,1)S(1)}, u32[]{:S(2)}, u32[]{:S(2)}) collective-permute-start(bf16[256,1,160]{0,2,1:T(8,128)(2,1)S(1)} %get-tuple-element.539), channel_id=1, source_target_pairs={{0,8},{8,16},{16,24},{24,32},{32,40},{40,48},{48,56},{56,64},{64,7... | collective-permute-start | bytes 245768 | tf_op jit(solution)/shard_map/while/body/eval_jaxpr/ppermute | solution.py:19
  84.9 14.5 %collective-permute-start = (bf16[256,1,160]{0,2,1:T(8,128)(2,1)S(1)}, bf16[256,1,160]{0,2,1:T(8,128)(2,1)S(1)}, u32[]{:S(2)}, u32[]{:S(2)}) collective-permute-start(bf16[256,1,160]{0,2,1:T(8,128)(2,1)S(1)} %get-tuple-element.539), channel_id=1, source_target_pairs={{0,8},{8,16},{16,24},{24,32},{32,40},{40,48},{48,56},{56,64},{64,7... | collective-permute-start | bytes 245768 | tf_op jit(solution)/shard_map/while/body/eval_jaxpr/ppermute | solution.py:19
  100.0 14.5 %collective-permute-start = (bf16[256,1,160]{0,2,1:T(8,128)(2,1)S(1)}, bf16[256,1,160]{0,2,1:T(8,128)(2,1)S(1)}, u32[]{:S(2)}, u32[]{:S(2)}) collective-permute-start(bf16[256,1,160]{0,2,1:T(8,128)(2,1)S(1)} %get-tuple-element.539), channel_id=1, source_target_pairs={{0,8},{8,16},{16,24},{24,32},{32,40},{40,48},{48,56},{56,64},{64,7... | collective-permute-start | bytes 245768 | tf_op jit(solution)/shard_map/while/body/eval_jaxpr/ppermute | solution.py:19
  115.2 14.5 %collective-permute-start = (bf16[256,1,160]{0,2,1:T(8,128)(2,1)S(1)}, bf16[256,1,160]{0,2,1:T(8,128)(2,1)S(1)}, u32[]{:S(2)}, u32[]{:S(2)}) collective-permute-start(bf16[256,1,160]{0,2,1:T(8,128)(2,1)S(1)} %get-tuple-element.539), channel_id=1, source_target_pairs={{0,8},{8,16},{16,24},{24,32},{32,40},{40,48},{48,56},{56,64},{64,7... | collective-permute-start | bytes 245768 | tf_op jit(solution)/shard_map/while/body/eval_jaxpr/ppermute | solution.py:19
  130.4 14.6 %collective-permute-start = (bf16[256,1,160]{0,2,1:T(8,128)(2,1)S(1)}, bf16[256,1,160]{0,2,1:T(8,128)(2,1)S(1)}, u32[]{:S(2)}, u32[]{:S(2)}) collective-permute-start(bf16[256,1,160]{0,2,1:T(8,128)(2,1)S(1)} %get-tuple-element.539), channel_id=1, source_target_pairs={{0,8},{8,16},{16,24},{24,32},{32,40},{40,48},{48,56},{56,64},{64,7... | collective-permute-start | bytes 245768 | tf_op jit(solution)/shard_map/while/body/eval_jaxpr/ppermute | solution.py:19
  151.2 2.1 copy-start.2
  152.0 2.6 copy-start.8
  152.0 2.6 copy-start.9
  154.6 190.7 %copy-start.13 = (pred[256]{0:T(512)(128)(4,1)S(1)}, pred[256]{0:T(512)(128)(4,1)}, u32[]{:S(2)}) copy-start(pred[256]{0:T(512)(128)(4,1)} %copy-done.12) | copy-start | bytes 772
  178.3 23.4 %copy-start.5 = (bf16[4,256,80]{1,2,0:T(8,128)(2,1)S(1)}, bf16[4,256,80]{1,2,0:T(8,128)(2,1)}, u32[]{:S(2)}) copy-start(bf16[4,256,80]{1,2,0:T(8,128)(2,1)} %get-tuple-element.564) | copy-start | bytes 491524 | tf_op jit(solution)/shard_map/while
  201.7 0.7 copy-start.6
  225.9 23.4 %copy-start.5 = (bf16[4,256,80]{1,2,0:T(8,128)(2,1)S(1)}, bf16[4,256,80]{1,2,0:T(8,128)(2,1)}, u32[]{:S(2)}) copy-start(bf16[4,256,80]{1,2,0:T(8,128)(2,1)} %get-tuple-element.564) | copy-start | bytes 491524 | tf_op jit(solution)/shard_map/while
  249.3 0.7 copy-start.6
  273.6 23.4 %copy-start.5 = (bf16[4,256,80]{1,2,0:T(8,128)(2,1)S(1)}, bf16[4,256,80]{1,2,0:T(8,128)(2,1)}, u32[]{:S(2)}) copy-start(bf16[4,256,80]{1,2,0:T(8,128)(2,1)} %get-tuple-element.564) | copy-start | bytes 491524 | tf_op jit(solution)/shard_map/while
  297.0 0.7 copy-start.6
  321.3 23.4 %copy-start.5 = (bf16[4,256,80]{1,2,0:T(8,128)(2,1)S(1)}, bf16[4,256,80]{1,2,0:T(8,128)(2,1)}, u32[]{:S(2)}) copy-start(bf16[4,256,80]{1,2,0:T(8,128)(2,1)} %get-tuple-element.564) | copy-start | bytes 491524 | tf_op jit(solution)/shard_map/while
  344.7 0.7 copy-start.6
where the time goes:
time: 352 us; the launch traced here: 348 us
  local copies, waits for them, and re-layouts  133 us (38%)
  waiting for transfers between devices  101 us (29%)
  matrix products  47.7 us (14%)
  other arithmetic  33.7 us (10%)
  starting transfers between devices  22.2 us (6%)
  loops' own time  10.4 us (3%)
    ppermute x8, waiting for transfers between devices, passed_along(): return lax.ppermute(x, axis, pairs)  101 us
    squeeze x72, local copies, waits for them, and re-layouts, one_head(): scores = lax.map(score_tile, (head_kv, allowed, key_segment))  66.2 us
    dynamic_slice x72, local copies, waits for them, and re-layouts, one_head(): lax.scan(value_step, start_state, (scores, head_kv, allowed, key_segment))  39.8 us
    dot_general x36, matrix products, score_tile(): lax.dot_general(head_queries, kv_block[:, :HD], (((1,), (1,)), ((), ())),...  32.6 us
    ppermute x8, starting transfers between devices, passed_along(): return lax.ppermute(x, axis, pairs)  16.8 us
    dot_general x36, matrix products, value_step(): jnp.dot(weights, kv_block[:, HD:], preferred_element_type=jnp.float32)  11 us
    another operation x1, loops' own time, per_device(): per_head = lax.map(one_head, jnp.arange(head_total, dtype=jnp.int32))  8.12 us
    reduce_max x4, other arithmetic, one_head(): row_max = jnp.max(jnp.max(scores, axis=-1), axis=0)  7.93 us
  transfers between devices with their start and end apart: 9, of which 8 were waited for; matrix products, arithmetic and copies ran while one was open for 57% of the time, Pallas kernels for 0%

commit v1 on v0

--- a/solution.py
+++ b/solution.py
@@ -86,70 +86,34 @@
     head_total = kv_heads * group_size
     packed = jnp.concatenate([key_rot, value_rows], axis=-1)
 
-    def relay(held_block, unused):
-        arrived = passed_along(held_block, "req", 1)
-        return (arrived, arrived)
-
-    unused_last, earlier_stack = lax.scan(relay, packed, None, length=reach_blocks)
-    key_blocks = jnp.concatenate([earlier_stack[::-1], packed[None]], axis=0)
-    key_index = (
-        block_start
-        - reach_blocks * row_count
-        + jnp.arange((reach_blocks + 1) * row_count, dtype=jnp.int32)
-    )
+    earlier = [passed_along(packed, "req", shift) for shift in range(reach_blocks, 0, -1)]
+    key_blocks = jnp.concatenate(earlier + [packed], axis=0)
+    key_count = (reach_blocks + 1) * row_count
+    key_index = block_start - reach_blocks * row_count + jnp.arange(key_count, dtype=jnp.int32)
     key_segment, unused_position, key_live = token_meta(key_index, page_counts, pad_counts)
-    key_index = key_index.reshape(reach_blocks + 1, row_count)
-    key_segment = key_segment.reshape(reach_blocks + 1, row_count)
-    key_live = key_live.reshape(reach_blocks + 1, row_count)
-    allowed = (key_segment[:, None, :] == segment_id[None, :, None]) & key_live[:, None, :]
+    allowed = (key_segment[None, :] == segment_id[:, None]) & key_live[None, :]
     allowed = (
         allowed
-        & (key_index[:, None, :] <= slot_index[None, :, None])
-        & (slot_index[None, :, None] - key_index[:, None, :] < WINDOW)
+        & (key_index[None, :] <= slot_index[:, None])
+        & (slot_index[:, None] - key_index[None, :] < WINDOW)
     )
     score_scale = HD ** (-0.5)
-
-    def one_head(head_id):
-        kv_id = head_id // group_size
-        head_queries = lax.dynamic_index_in_dim(query_rot, head_id, 1, keepdims=False)
-        head_kv = lax.dynamic_index_in_dim(key_blocks, kv_id, 2, keepdims=False)
-
-        def score_tile(inputs):
-            kv_block, block_allowed, block_segment = inputs
-            tile = (
-                lax.dot_general(
-                    head_queries,
-                    kv_block[:, :HD],
-                    (((1,), (1,)), ((), ())),
-                    preferred_element_type=jnp.float32,
-                )
-                * score_scale
-            )
-            return jnp.where(block_allowed, tile, MASKED_SCORE)
-
-        scores = lax.map(score_tile, (head_kv, allowed, key_segment))
-        row_max = jnp.max(jnp.max(scores, axis=-1), axis=0)
-
-        def value_step(state, inputs):
-            block_scores, kv_block, block_allowed, block_segment = inputs
-            prob_total, weighted = state
-            probs = jnp.where(block_allowed, jnp.exp(block_scores - row_max[:, None]), 0.0)
-            weights = probs.astype(jnp.bfloat16)
-            update = jnp.dot(weights, kv_block[:, HD:], preferred_element_type=jnp.float32)
-            return ((prob_total + jnp.sum(probs, axis=-1), weighted + update), None)
-
-        start_state = (
-            jnp.zeros((row_count,), jnp.float32),
-            jnp.zeros((row_count, HD), jnp.float32),
-        )
-        final_state, unused_rest = lax.scan(
-            value_step, start_state, (scores, head_kv, allowed, key_segment)
-        )
-        prob_total, weighted = final_state
-        return weighted / prob_total[:, None]
-
-    per_head = lax.map(one_head, jnp.arange(head_total, dtype=jnp.int32))
-    result = jnp.transpose(per_head, (1, 0, 2)).reshape(row_count, head_total * HD)
+    queries = query_rot.reshape(row_count, kv_heads, group_size, HD)
+    keys = key_blocks[..., :HD]
+    values = key_blocks[..., HD:]
+    scores = (
+        jnp.einsum("tgjd,ugd->gjtu", queries, keys, preferred_element_type=jnp.float32)
+        * score_scale
+    )
+    scores = jnp.where(allowed[None, None], scores, MASKED_SCORE)
+    row_max = jnp.max(scores, axis=-1, keepdims=True)
+    probs = jnp.where(allowed[None, None], jnp.exp(scores - row_max), 0.0)
+    prob_total = jnp.sum(probs, axis=-1)
+    weights = probs.astype(jnp.bfloat16)
+    weighted = jnp.einsum("gjtu,ugd->tgjd", weights, values, preferred_element_type=jnp.float32)
+    result = (weighted / jnp.transpose(prob_total, (2, 0, 1))[..., None]).reshape(
+        row_count, head_total * HD
+    )
     context = jnp.where(is_live[:, None], result, 0.0).astype(jnp.bfloat16)
     live_rows = jnp.where(is_live[:, None, None], packed, jnp.zeros((), jnp.bfloat16))
     page_total = row_count // PAGE

time: 352 us -> 94.1 us (0.27)
  local copies, waits for them, and re-layouts: 133 us -> 6.49 us
  waiting for transfers between devices: 101 us -> 36.4 us
  matrix products: 47.7 us -> 8.32 us
  other arithmetic: 33.7 us -> 9.68 us
  loops' own time: 10.4 us -> 0 us
  starting transfers between devices: 22.2 us -> 31.6 us
    squeeze x76 -> x0, local copies, waits for them, and re-layouts: 66.3 us -> none  [the longest x72 66.2 us: one_head(): scores = lax.map(score_tile, (head_kv, allowed, key_segment))]
    ppermute x8, waiting for transfers between devices: 101 us -> 36.4 us  [passed_along(): return lax.ppermute(x, axis, pairs)]
    dynamic_slice x148 -> x0, local copies, waits for them, and re-layouts: 47.4 us -> none  [the longest x72 39.8 us: one_head(): lax.scan(value_step, start_state, (scores, head_kv, allowed, key_segment))]
    dot_general x72 -> x2, matrix products: 43.6 us -> 4.29 us  [the longest x1 2.61 us: per_device(): jnp.einsum('gjtu,ugd->tgjd', weights, values, preferred_element_type=jnp....]
    another operation x10 -> x0, loops' own time: 10.4 us -> none  [the longest x1 8.12 us: per_device(): per_head = lax.map(one_head, jnp.arange(head_total, dtype=jnp.int32))]
    ppermute x8, starting transfers between devices: 16.8 us -> 26.8 us  [passed_along(): return lax.ppermute(x, axis, pairs)]
    reduce_max x4 -> x0, other arithmetic: 7.93 us -> none  [one_head(): row_max = jnp.max(jnp.max(scores, axis=-1), axis=0)]
    dynamic_update_slice x8 -> x0, local copies, waits for them, and re-layouts: 5.09 us -> none  [per_device(): lax.scan(relay, packed, None, length=reach_blocks)]
  transfers between devices with their start and end apart: 9 -> 9, of which waited for: 8 -> 3; matrix products, arithmetic and copies ran while one was open for 57% -> 19% of each run, Pallas kernels for 0% -> 0%
where the time goes in v1:
time: 94.1 us; the launch traced here: 93.4 us
  waiting for transfers between devices  36.4 us (39%)
  starting transfers between devices  31.6 us (34%)
  other arithmetic  9.68 us (10%)
  matrix products  8.32 us (9%)
  local copies, waits for them, and re-layouts  6.49 us (7%)
  between operations  0.97 us (1%)
    ppermute x8, waiting for transfers between devices, passed_along(): return lax.ppermute(x, axis, pairs)  36.4 us
    ppermute x8, starting transfers between devices, passed_along(): return lax.ppermute(x, axis, pairs)  26.8 us
    all_to_all x1, starting transfers between devices, per_device(): lax.all_to_all(outgoing, 'tp', split_axis=1, concat_axis=1, tiled=True)  4.73 us
    unnamed x21, local copies, waits for them, and re-layouts  4.29 us
    dot_general x1, matrix products, per_device(): jnp.einsum('gjtu,ugd->tgjd', weights, values, preferred_element_type=jnp....  2.61 us
    reduce_sum x1, other arithmetic, per_device(): prob_total = jnp.sum(probs, axis=-1)  2.31 us
    and x1, other arithmetic, per_device(): allowed & (key_index[None, :] <= slot_index[:, None])  2.16 us
    dot_general x1, matrix products, project(): jnp.dot(normed, w_value, preferred_element_type=jnp.float32)  2.02 us
  transfers between devices with their start and end apart: 9, of which 3 were waited for; matrix products, arithmetic and copies ran while one was open for 19% of the time, Pallas kernels for 0%

profile of v1, /device:TPU:192, one launch (start us, length us, event | category | flops | bytes accessed | tf_op | source)
XLA Modules:
  0.0 93.4 jit_solution(17755424469995205289)
XLA Ops:
  0.6 0.0 copy-start
  0.6 0.0 copy-start.1
  0.7 0.0 copy-start.4
  0.7 0.8 fusion.40
  1.5 1.7 %fusion.7 = f32[256]{0:T(256)S(1)} fusion(bf16[256,2560]{1,0:T(8,128)(2,1)} %param.8), kind=kLoop, calls=%fused_computation.11 | loop fusion | flops 1965824 | bytes 1311744 | tf_op jit(solution)/shard_map/reduce_sum | solution.py:58
  3.2 0.0 copy-start.2
  3.2 0.1 copy.23
  3.3 0.1 reduce.2
  3.5 0.0 copy-start.3
  3.5 0.1 convert_reduce_fusion.1
  3.6 0.7 fusion.39
  4.3 0.1 select_reduce_fusion.2
  4.4 0.0 copy-start.5
  4.4 2.0 %fusion.14 = bf16[256,1,80]{0,2,1:T(8,128)(2,1)S(1)} fusion(bf16[2560,80]{0,1:T(8,128)(2,1)} %param.12, bf16[256,2560]{1,0:T(8,128)(2,1)} %param.8, f32[2560]{0:T(1024)} %param.9, f32[256]{0:T(256)S(1)} %add_rsqrt_fusion), kind=kOutput, calls=%fused_computation.19 | convolution fusion | flops 107499520 | bytes 1772544 | tf_op jit(solution)/shard_map/dot_general | solution.py:68
  6.4 0.0 copy-done.2
  6.4 0.0 copy-done.1
  6.4 0.0 copy-done.4
  6.4 0.0 copy-done.3
  6.4 0.6 convolution_bitcast_fusion
  7.0 0.2 fusion.28
  7.3 3.5 %collective-permute-start.7 = (bf16[256,1,160]{0,2,1:T(8,128)(2,1)S(1)}, bf16[256,1,160]{0,2,1:T(8,128)(2,1)S(1)}, u32[]{:S(2)}, u32[]{:S(2)}) collective-permute-start(bf16[256,1,160]{0,2,1:T(8,128)(2,1)S(1)} %pad_maximum_fusion), channel_id=1, source_target_pairs={{0,8},{8,16},{16,24},{24,32},{32,40},{40,48},{48,56},{56,64},{64,7... | collective-permute-start | bytes 245768 | tf_op jit(solution)/shard_map/ppermute | solution.py:19
  10.8 4.8 %collective-permute-start.6 = (bf16[256,1,160]{0,2,1:T(8,128)(2,1)S(1)}, bf16[256,1,160]{0,2,1:T(8,128)(2,1)}, u32[]{:S(2)}, u32[]{:S(2)}) collective-permute-start(bf16[256,1,160]{0,2,1:T(8,128)(2,1)S(1)} %pad_maximum_fusion), channel_id=1, source_target_pairs={{0,16},{8,24},{16,32},{24,40},{32,48},{40,56},{48,64},{56,72},{64,... | collective-permute-start | bytes 245768 | tf_op jit(solution)/shard_map/ppermute | solution.py:19
  15.6 4.2 %collective-permute-start.5 = (bf16[256,1,160]{0,2,1:T(8,128)(2,1)S(1)}, bf16[256,1,160]{0,2,1:T(8,128)(2,1)}, u32[]{:S(2)}, u32[]{:S(2)}) collective-permute-start(bf16[256,1,160]{0,2,1:T(8,128)(2,1)S(1)} %pad_maximum_fusion), channel_id=1, source_target_pairs={{0,24},{8,32},{16,40},{24,48},{32,56},{40,64},{48,72},{56,80},{64,... | collective-permute-start | bytes 245768 | tf_op jit(solution)/shard_map/ppermute | solution.py:19
  19.8 3.4 %collective-permute-start.4 = (bf16[256,1,160]{0,2,1:T(8,128)(2,1)S(1)}, bf16[256,1,160]{0,2,1:T(8,128)(2,1)}, u32[]{:S(2)}, u32[]{:S(2)}) collective-permute-start(bf16[256,1,160]{0,2,1:T(8,128)(2,1)S(1)} %pad_maximum_fusion), channel_id=1, source_target_pairs={{0,32},{8,40},{16,48},{24,56},{32,64},{40,72},{48,80},{56,88},{64,... | collective-permute-start | bytes 245768 | tf_op jit(solution)/shard_map/ppermute | solution.py:19
  23.2 3.2 %collective-permute-start = (bf16[256,1,160]{0,2,1:T(8,128)(2,1)S(1)}, bf16[256,1,160]{0,2,1:T(8,128)(2,1)}, u32[]{:S(2)}, u32[]{:S(2)}) collective-permute-start(bf16[256,1,160]{0,2,1:T(8,128)(2,1)S(1)} %pad_maximum_fusion), channel_id=1, source_target_pairs={{0,64},{8,72},{16,80},{24,88},{32,96},{40,104},{48,112},{56,120},{... | collective-permute-start | bytes 245768 | tf_op jit(solution)/shard_map/ppermute | solution.py:19
  26.4 0.1 copy.25
  26.5 0.0 copy-done.5
  26.5 0.1 select_reduce_fusion.4
  26.6 0.1 reshape.428
  26.7 0.1 copy.26
  26.8 0.1 reshape.434
  26.9 0.1 broadcast_in_dim.61
  27.0 0.2 broadcast_in_dim.96
  27.2 0.2 concatenate.32
  27.4 0.6 gather_fusion
  28.0 0.7 copy.27
  28.7 4.7 %all-to-all-start = ((bf16[2,8,2560]{2,0,1:T(2,128)(2,1)}), bf16[2,8,2560]{2,0,1:T(2,128)(2,1)S(1)}, u32[]{:S(2)}, u32[]{:S(2)}) async-start(bf16[2,8,2560]{2,0,1:T(2,128)(2,1)} %copy.27), calls=%async_computation | async-start | bytes 163840 | tf_op jit(solution)/shard_map/all_to_all | solution.py:134
  33.4 0.1 convert_reduce_fusion
  33.5 0.1 select_reduce_fusion.1
  33.7 0.2 multiply_cosine_fusion
  33.9 0.0 copy-done
  33.9 1.4 %fusion.45 = f32[256,320]{0,1:T(8,128)S(1)} fusion(bf16[2560,320]{0,1:T(8,128)(2,1)S(1)} %copy-done, bf16[256,2560]{1,0:T(8,128)(2,1)S(1)} %copy-done.1, f32[2560]{0:T(1024)} %param.9, f32[256]{0:T(256)} %copy-done.2), kind=kOutput, calls=%fused_computation.87 | convolution fusion | flops 422051840 | bytes 3288064 | tf_op jit(solution)/shard_map/dot_general | solution.py:61
  35.3 2.2 %fusion.10 = pred[256,2304]{0,1:T(8,128)(4,1)S(1)} fusion(s32[256]{0:T(256)S(1)} %iota_add_fusion.1, s32[256]{0:T(256)S(1)} %fusion.36, s32[2304]{0:T(1024)S(1)} %iota_add_fusion, s32[2304]{0:T(1024)S(1)} %fusion.33, pred[2304]{0:T(1024)(128)(4,1)S(1)} %fusion.31), kind=kLoop, calls=%fused_computation.15 | loop fusion | flops 4128768 | bytes 612608 | tf_op jit(solution)/shard_map/and | solution.py:96
  37.6 0.0 collective-permute-done
  37.6 3.3 %collective-permute-start.1 = (bf16[256,1,160]{0,2,1:T(8,128)(2,1)S(1)}, bf16[256,1,160]{0,2,1:T(8,128)(2,1)S(1)}, u32[]{:S(2)}, u32[]{:S(2)}) collective-permute-start(bf16[256,1,160]{0,2,1:T(8,128)(2,1)S(1)} %pad_maximum_fusion), channel_id=1, source_target_pairs={{0,56},{8,64},{16,72},{24,80},{32,88},{40,96},{48,104},{56,112},{6... | collective-permute-start | bytes 245768 | tf_op jit(solution)/shard_map/ppermute | solution.py:19
  40.9 0.9 constant_dynamic-update-slice_fusion.8
  41.8 11.0 %collective-permute-done.1 = bf16[256,1,160]{0,2,1:T(8,128)(2,1)S(1)} collective-permute-done((bf16[256,1,160]{0,2,1:T(8,128)(2,1)S(1)}, bf16[256,1,160]{0,2,1:T(8,128)(2,1)S(1)}, u32[]{:S(2)}, u32[]{:S(2)}) %collective-permute-start.1) | collective-permute-done | bytes 81952 | tf_op jit(solution)/shard_map/ppermute | solution.py:19
  52.7 1.9 %collective-permute-start.2 = (bf16[256,1,160]{0,2,1:T(8,128)(2,1)S(1)}, bf16[256,1,160]{0,2,1:T(8,128)(2,1)S(1)}, u32[]{:S(2)}, u32[]{:S(2)}) collective-permute-start(bf16[256,1,160]{0,2,1:T(8,128)(2,1)S(1)} %pad_maximum_fusion), channel_id=1, source_target_pairs={{0,48},{8,56},{16,64},{24,72},{32,80},{40,88},{48,96},{56,104},{64... | collective-permute-start | bytes 245768 | tf_op jit(solution)/shard_map/ppermute | solution.py:19
  54.7 13.2 %collective-permute-done.2 = bf16[256,1,160]{0,2,1:T(8,128)(2,1)S(1)} collective-permute-done((bf16[256,1,160]{0,2,1:T(8,128)(2,1)S(1)}, bf16[256,1,160]{0,2,1:T(8,128)(2,1)S(1)}, u32[]{:S(2)}, u32[]{:S(2)}) %collective-permute-start.2) | collective-permute-done | bytes 81952 | tf_op jit(solution)/shard_map/ppermute | solution.py:19
  67.9 2.6 %collective-permute-start.3 = (bf16[256,1,160]{0,2,1:T(8,128)(2,1)S(1)}, bf16[256,1,160]{0,2,1:T(8,128)(2,1)S(1)}, u32[]{:S(2)}, u32[]{:S(2)}) collective-permute-start(bf16[256,1,160]{0,2,1:T(8,128)(2,1)S(1)} %pad_maximum_fusion), channel_id=1, source_target_pairs={{0,40},{8,48},{16,56},{24,64},{32,72},{40,80},{48,88},{56,96},{64,... | collective-permute-start | bytes 245768 | tf_op jit(solution)/shard_map/ppermute | solution.py:19
  70.5 12.2 %collective-permute-done.3 = bf16[256,1,160]{0,2,1:T(8,128)(2,1)S(1)} collective-permute-done((bf16[256,1,160]{0,2,1:T(8,128)(2,1)S(1)}, bf16[256,1,160]{0,2,1:T(8,128)(2,1)S(1)}, u32[]{:S(2)}, u32[]{:S(2)}) %collective-permute-start.3) | collective-permute-done | bytes 81952 | tf_op jit(solution)/shard_map/ppermute | solution.py:19
  82.7 0.0 collective-permute-done.4
  82.7 0.9 constant_dynamic-update-slice_fusion.4
  83.6 0.0 collective-permute-done.5
  83.6 0.9 constant_dynamic-update-slice_fusion.3
  84.5 0.0 collective-permute-done.6
  84.5 0.9 constant_dynamic-update-slice_fusion.2
  85.4 0.0 collective-permute-done.7
  85.4 1.7 %fusion = (f32[4,256]{1,0:T(4,128)S(1)}, f32[2304,256,4]{1,0,2:T(8,128)S(1)}) fusion(pred[256,2304]{0,1:T(8,128)(4,1)S(1)} %fusion.10, bf16[256,4,40]{0,2,1:T(8,128)(2,1)S(1)} %get-tuple-element.11, bf16[256,4,40]{0,2,1:T(8,128)(2,1)S(1)} %get-tuple-element.10, bf16[2304,1,160]{0,2,1:T(8,128)(2,1)S(1)} %constant_dynamic-update-slice_fusion), kind=kOutput, calls=%fused_computation.3 | convolution fusion | flops 384891904 | bytes 10563584 | tf_op jit(solution)/shard_map/tgjd,ugd->gjtu/dot_general | solution.py:105
  87.1 2.3 %fusion.1 = f32[4,256]{1,0:T(4,128)S(1)} fusion(f32[2304,256,4]{1,0,2:T(8,128)S(1)} %get-tuple-element.19, f32[4,256]{1,0:T(4,128)S(1)} %get-tuple-element.18, pred[256,2304]{0,1:T(8,128)(4,1)S(1)} %fusion.10), kind=kLoop, calls=%fused_computation.4 | loop fusion | flops 11795456 | bytes 10035200 | tf_op jit(solution)/shard_map/reduce_sum | solution.py:111
  89.4 2.6 %fusion.15 = bf16[256,1,4,80]{0,3,2,1:T(8,128)(2,1)S(1)} fusion(f32[2304,256,4]{1,0,2:T(8,128)S(1)} %get-tuple-element.19, f32[4,256]{1,0:T(4,128)S(1)} %get-tuple-element.18, pred[256,2304]{0,1:T(8,128)(4,1)S(1)} %fusion.10, bf16[2304,1,160]{0,2,1:T(8,128)(2,1)S(1)} %constant_dynamic-update-slice_fusion, f32[256,4]{0,1:T(4,128)S(1)} %bitcast.75), kind=kOutput, calls=%fused_computation.20 | convolution fusion | flops 389447680 | bytes 10567680 | tf_op jit(solution)/shard_map/gjtu,ugd->tgjd/dot_general | solution.py:113
  92.1 0.7 fusion.19
  92.8 0.0 all-to-all-done
  92.8 0.6 copy.28
  (20 shorter events, 0.2 us)
Async XLA Ops:
  0.6 33.3 %copy-start = (bf16[2560,320]{0,1:T(8,128)(2,1)S(1)}, bf16[2560,320]{0,1:T(8,128)(2,1)}, u32[]{:S(2)}) copy-start(bf16[2560,320]{0,1:T(8,128)(2,1)} %param.10) | copy-start | bytes 4915204
  0.6 5.7 %copy-start.1 = (bf16[256,2560]{1,0:T(8,128)(2,1)S(1)}, bf16[256,2560]{1,0:T(8,128)(2,1)}, u32[]{:S(2)}) copy-start(bf16[256,2560]{1,0:T(8,128)(2,1)} %param.8) | copy-start | bytes 3932164
  0.7 5.7 %copy-start.4 = (f32[2560]{0:T(1024)S(1)}, f32[2560]{0:T(1024)}, u32[]{:S(2)}) copy-start(f32[2560]{0:T(1024)} %param.9) | copy-start | bytes 30724
  3.2 3.2 %copy-start.2 = (f32[256]{0:T(256)}, f32[256]{0:T(256)S(1)}, u32[]{:S(2)}) copy-start(f32[256]{0:T(256)S(1)} %add_rsqrt_fusion) | copy-start | bytes 3076
  3.5 3.0 %copy-start.3 = (bf16[2560,80]{0,1:T(8,128)(2,1)S(1)}, bf16[2560,80]{0,1:T(8,128)(2,1)}, u32[]{:S(2)}) copy-start(bf16[2560,80]{0,1:T(8,128)(2,1)} %param.11) | copy-start | bytes 1228804
  4.4 22.1 %copy-start.5 = (s32[1,16]{1,0:T(1,128)S(1)}, s32[1,16]{1,0:T(1,128)}, u32[]{:S(2)}) copy-start(s32[1,16]{1,0:T(1,128)} %param.15) | copy-start | bytes 196
  7.3 78.1 %collective-permute-start.7 = (bf16[256,1,160]{0,2,1:T(8,128)(2,1)S(1)}, bf16[256,1,160]{0,2,1:T(8,128)(2,1)S(1)}, u32[]{:S(2)}, u32[]{:S(2)}) collective-permute-start(bf16[256,1,160]{0,2,1:T(8,128)(2,1)S(1)} %pad_maximum_fusion), channel_id=1, source_target_pairs={{0,8},{8,16},{16,24},{24,32},{32,40},{40,48},{48,56},{56,64},{64,7... | collective-permute-start | bytes 245768 | tf_op jit(solution)/shard_map/ppermute | solution.py:19
  10.8 73.7 %collective-permute-start.6 = (bf16[256,1,160]{0,2,1:T(8,128)(2,1)S(1)}, bf16[256,1,160]{0,2,1:T(8,128)(2,1)}, u32[]{:S(2)}, u32[]{:S(2)}) collective-permute-start(bf16[256,1,160]{0,2,1:T(8,128)(2,1)S(1)} %pad_maximum_fusion), channel_id=1, source_target_pairs={{0,16},{8,24},{16,32},{24,40},{32,48},{40,56},{48,64},{56,72},{64,... | collective-permute-start | bytes 245768 | tf_op jit(solution)/shard_map/ppermute | solution.py:19
  15.6 68.0 %collective-permute-start.5 = (bf16[256,1,160]{0,2,1:T(8,128)(2,1)S(1)}, bf16[256,1,160]{0,2,1:T(8,128)(2,1)}, u32[]{:S(2)}, u32[]{:S(2)}) collective-permute-start(bf16[256,1,160]{0,2,1:T(8,128)(2,1)S(1)} %pad_maximum_fusion), channel_id=1, source_target_pairs={{0,24},{8,32},{16,40},{24,48},{32,56},{40,64},{48,72},{56,80},{64,... | collective-permute-start | bytes 245768 | tf_op jit(solution)/shard_map/ppermute | solution.py:19
  19.8 62.9 %collective-permute-start.4 = (bf16[256,1,160]{0,2,1:T(8,128)(2,1)S(1)}, bf16[256,1,160]{0,2,1:T(8,128)(2,1)}, u32[]{:S(2)}, u32[]{:S(2)}) collective-permute-start(bf16[256,1,160]{0,2,1:T(8,128)(2,1)S(1)} %pad_maximum_fusion), channel_id=1, source_target_pairs={{0,32},{8,40},{16,48},{24,56},{32,64},{40,72},{48,80},{56,88},{64,... | collective-permute-start | bytes 245768 | tf_op jit(solution)/shard_map/ppermute | solution.py:19
  23.2 14.4 %collective-permute-start = (bf16[256,1,160]{0,2,1:T(8,128)(2,1)S(1)}, bf16[256,1,160]{0,2,1:T(8,128)(2,1)}, u32[]{:S(2)}, u32[]{:S(2)}) collective-permute-start(bf16[256,1,160]{0,2,1:T(8,128)(2,1)S(1)} %pad_maximum_fusion), channel_id=1, source_target_pairs={{0,64},{8,72},{16,80},{24,88},{32,96},{40,104},{48,112},{56,120},{... | collective-permute-start | bytes 245768 | tf_op jit(solution)/shard_map/ppermute | solution.py:19
  28.7 64.1 %all-to-all-start = ((bf16[2,8,2560]{2,0,1:T(2,128)(2,1)}), bf16[2,8,2560]{2,0,1:T(2,128)(2,1)S(1)}, u32[]{:S(2)}, u32[]{:S(2)}) async-start(bf16[2,8,2560]{2,0,1:T(2,128)(2,1)} %copy.27), calls=%async_computation | async-start | bytes 163840 | tf_op jit(solution)/shard_map/all_to_all | solution.py:134
  37.6 15.1 %collective-permute-start.1 = (bf16[256,1,160]{0,2,1:T(8,128)(2,1)S(1)}, bf16[256,1,160]{0,2,1:T(8,128)(2,1)S(1)}, u32[]{:S(2)}, u32[]{:S(2)}) collective-permute-start(bf16[256,1,160]{0,2,1:T(8,128)(2,1)S(1)} %pad_maximum_fusion), channel_id=1, source_target_pairs={{0,56},{8,64},{16,72},{24,80},{32,88},{40,96},{48,104},{56,112},{6... | collective-permute-start | bytes 245768 | tf_op jit(solution)/shard_map/ppermute | solution.py:19
  52.7 15.1 %collective-permute-start.2 = (bf16[256,1,160]{0,2,1:T(8,128)(2,1)S(1)}, bf16[256,1,160]{0,2,1:T(8,128)(2,1)S(1)}, u32[]{:S(2)}, u32[]{:S(2)}) collective-permute-start(bf16[256,1,160]{0,2,1:T(8,128)(2,1)S(1)} %pad_maximum_fusion), channel_id=1, source_target_pairs={{0,48},{8,56},{16,64},{24,72},{32,80},{40,88},{48,96},{56,104},{64... | collective-permute-start | bytes 245768 | tf_op jit(solution)/shard_map/ppermute | solution.py:19
  67.9 14.8 %collective-permute-start.3 = (bf16[256,1,160]{0,2,1:T(8,128)(2,1)S(1)}, bf16[256,1,160]{0,2,1:T(8,128)(2,1)S(1)}, u32[]{:S(2)}, u32[]{:S(2)}) collective-permute-start(bf16[256,1,160]{0,2,1:T(8,128)(2,1)S(1)} %pad_maximum_fusion), channel_id=1, source_target_pairs={{0,40},{8,48},{16,56},{24,64},{32,72},{40,80},{48,88},{56,96},{64,... | collective-permute-start | bytes 245768 | tf_op jit(solution)/shard_map/ppermute | solution.py:19
